TPU v7x, 512 devices: a whole 4x4x16 slice. The times are simulated.
512 devices in a mesh: section: 8 (over x, y_hi), vocab: 64 (over z, y_lo, core).
Axes of the slice: x: 4, y: 4 (y_hi: 2, y_lo: 2; y = y_hi * 2 + y_lo), z: 16, core: 2. Of those that a mesh axis runs over, the one named last changes fastest.
Arguments:
- hidden: bfloat16 [512, 8192], P('vocab', 'section'), may hold values from -6 to 6
- head_weight: bfloat16 [98304, 8192], P('vocab', 'section'), may hold values from -3 to 3
- lengths: int32 [8], replicated, may hold values from 16 to 64
- pairing: int32 [4], replicated, may hold values from 0 to 3, each once
Outputs:
- hidden_grad: float32 [512, 8192], P('vocab', 'section')
- loss: float32 [], replicated
Inputs may be any that keep to these rules, and one draw needn't show every extreme that they name: Every sequence has at least one live token; positions from lengths on are padding. `pairing`: a permutation: each document matches exactly one query.
All inputs are finite; a program needn't handle non-finite values.
Results may differ from a plain program's by a relative error of at most 0.0018.
Values may be sent and summed in bfloat16 or wider, within the bound.
No kernel may reach another device: no remote copies, remote signals or barrier semaphores. Data moves between devices by JAX's collectives and lax.ppermute only.
A program may use at most 64 MiB of HBM per device.

v0:
```python
import jax
import jax.numpy as jnp
from jax import lax
from jax.sharding import Mesh
from jax.sharding import PartitionSpec as P

NSEQ = 8
pool_temp = 0.5
score_temp = 0.02
grad_scale = 16.0
eps_norm = 1e-06
SEC = ("x", "yh")
VOC = ("z", "yl", "c")


def local(hidden, head_weight, lengths, pairing):
    half = NSEQ // 2
    gathered = lax.all_gather(hidden, ("yl", "c"), axis=0, tiled=True)
    gathered = lax.all_gather(gathered, "z", axis=0, tiled=True)
    partial_logits = lax.dot_general(
        gathered, head_weight, (((1,), (1,)), ((), ())), preferred_element_type=jnp.float32
    )
    total_rows = partial_logits.shape[0]
    seq_len = total_rows // NSEQ
    logits = lax.psum_scatter(partial_logits, "x", scatter_dimension=1, tiled=True)
    logits = lax.psum_scatter(logits, "yh", scatter_dimension=1, tiled=True)
    columns = logits.shape[1]
    soft = jax.nn.softplus(logits)
    act = jnp.log1p(soft)
    positions = jnp.arange(seq_len, dtype=jnp.int32)
    live = (positions[None, :] < lengths[:, None]).astype(jnp.float32)
    expo = jnp.exp(act / pool_temp).reshape(NSEQ, seq_len, columns) * live[:, :, None]
    totals = jnp.sum(expo, axis=1)
    pooled = pool_temp * jnp.log(totals)
    queries = pooled[:half]
    documents = pooled[half:]
    dots_part = lax.dot_general(
        queries, documents, (((1,), (1,)), ((), ())), precision=lax.Precision.HIGHEST
    )
    norms_part = jnp.sum(pooled * pooled, axis=1)
    stats = (dots_part, norms_part)
    for axis in ("c", "yl", "yh", "x", "z"):
        stats = lax.psum(stats, axis)
    dots, norms = stats
    inv = lax.rsqrt(norms + eps_norm)
    inv_q = inv[:half]
    inv_d = inv[half:]
    scores = dots * inv_q[:, None] * inv_d[None, :] / score_temp
    weights = jnp.exp(scores)
    row_sum = jnp.sum(weights, axis=1)
    probs = weights / row_sum[:, None]
    target = (jnp.arange(half, dtype=jnp.int32)[None, :] == pairing[:, None]).astype(jnp.float32)
    loss = jnp.sum(jnp.log(row_sum) - jnp.sum(scores * target, axis=1))
    dscore = grad_scale * (probs - target)
    gdots = dscore * inv_q[:, None] * inv_d[None, :] / score_temp
    dinv_q = jnp.sum(dscore * dots * inv_d[None, :], axis=1) / score_temp
    dinv_d = jnp.sum(dscore * dots * inv_q[:, None], axis=0) / score_temp
    dinv = jnp.concatenate([dinv_q, dinv_d])
    dnorm = -0.5 * dinv * inv * inv * inv
    dpool_q = (
        jnp.dot(gdots, documents, precision=lax.Precision.HIGHEST)
        + 2.0 * dnorm[:half, None] * queries
    )
    dpool_d = (
        jnp.dot(gdots.T, queries, precision=lax.Precision.HIGHEST)
        + 2.0 * dnorm[half:, None] * documents
    )
    dpooled = jnp.concatenate([dpool_q, dpool_d], axis=0)
    dact = (dpooled[:, None, :] * expo / totals[:, None, :]).reshape(total_rows, columns)
    dlogit = (dact * jax.nn.sigmoid(logits) / (1.0 + soft)).astype(jnp.bfloat16)
    dlogit = lax.all_gather(dlogit, SEC, axis=1, tiled=True)
    partial_grad = jnp.dot(dlogit, head_weight, preferred_element_type=jnp.float32)
    hidden_grad = lax.psum_scatter(partial_grad, "z", scatter_dimension=0, tiled=True)
    hidden_grad = lax.psum_scatter(hidden_grad, ("yl", "c"), scatter_dimension=0, tiled=True)
    return (hidden_grad, loss)


def solution(mesh):
    n_sec, n_voc = mesh.devices.shape
    fine = Mesh(mesh.devices.reshape(n_sec // 2, 2, n_voc // 4, 2, 2), SEC + VOC)
    in_specs = (P(VOC, SEC), P(VOC, SEC), P(), P())
    out_specs = (P(VOC, SEC), P())
    return jax.shard_map(local, mesh=fine, in_specs=in_specs, out_specs=out_specs, check_vma=False)
```

profile of v0, /device:TPU:1, one launch (start us, length us, event | category | flops | bytes accessed | tf_op | source)
XLA Modules:
  0.0 403.5 jit_solution(7920873863289771938)
XLA Ops:
  7.2 0.0 copy-start
  7.2 0.0 all-gather.3.cloned.1.call-start
  7.2 12.7 %all_gather.9 = bf16[32,1024]{1,0:T(8,128)(2,1)} all-gather(bf16[8,1024]{1,0:T(8,128)(2,1)} %param.4), channel_id=1, replica_groups=mesh['x'=4,'yh'=2,'z'=16,'yl'=2,'c'=2] {'yl','c'}, dimensions={0}, use_global_device_ids=true | all-gather | bytes 81920 | tf_op jit(solution)/shard_map/all_gather | solution.py:18
  20.0 0.0 all-gather.3.cloned.1.call-update
  20.0 0.0 reduce-scatter.7.cloned.1.call-start
  20.0 60.9 %all-gather.3.cloned.1.call-done = bf16[512,1024]{1,0:T(8,128)(2,1)} async-done(((bf16[32,1024]{1,0:T(8,128)(2,1)}), bf16[512,1024]{1,0:T(8,128)(2,1)}) %all-gather.3.cloned.1.call-update) | async-done | bytes 1048592 | tf_op jit(solution)/shard_map/all_gather | solution.py:19
  81.0 0.0 copy-done
  81.0 4.7 %fusion.17 = f32[512,1536]{1,0:T(8,128)} fusion(bf16[512,1024]{1,0:T(8,128)(2,1)} %all-gather.3.cloned.1.call-done, bf16[1536,1024]{1,0:T(8,128)(2,1)S(1)} %copy-done), kind=kOutput, calls=%fused_computation.46 | convolution fusion | flops 1610612736 | bytes 7340032 | tf_op jit(solution)/shard_map/dot_general | solution.py:20
  85.7 0.0 copy-start.1
  85.7 0.0 copy-start.2
  85.7 0.0 reduce-scatter.7.cloned.1.call-update
  85.7 0.0 reduce-scatter.13.cloned.1.call-start
  85.8 52.5 %reduce-scatter.7.cloned.1.call-done = f32[512,384]{1,0:T(8,128)} async-done(((f32[512,1536]{1,0:T(8,128)}), f32[512,384]{1,0:T(8,128)}) %reduce-scatter.7.cloned.1.call-update) | async-done | bytes 786448 | tf_op jit(solution)/shard_map/reduce_scatter | solution.py:25
  138.3 2.3 copy.7
  140.6 0.0 reduce-scatter.13.cloned.1.call-update
  140.6 0.0 all-gather.5.cloned.1.call-start
  140.6 0.0 copy-done.1
  140.6 0.1 fusion.3
  140.7 0.1 reshape.50
  140.8 29.2 %reduce-scatter.13.cloned.1.call-done = f32[192,512]{1,0:T(8,128)} async-done(((f32[384,512]{1,0:T(8,128)}), f32[192,512]{1,0:T(8,128)}) %reduce-scatter.13.cloned.1.call-update) | async-done | bytes 393232
  170.0 2.0 copy.8
  172.0 1.6 multiply_reduce_fusion
  173.6 0.1 multiply_reduce_fusion.1
  173.7 0.1 fusion.5
  173.9 2.8 all-reduce.2
  176.6 3.8 all-reduce.3
  180.4 5.3 %all-reduce.4 = (f32[8]{0:T(128)S(1)}, f32[4,4]{1,0:T(4,128)S(1)}) all-reduce(f32[8]{0:T(128)S(1)} %get-tuple-element.11, f32[4,4]{1,0:T(4,128)S(1)} %get-tuple-element.12), channel_id=1, replica_groups=mesh['x'=4,'yh'=2,'z'=16,'yl'=2,'c'=2] {'yh'}, use_global_device_ids=true, to_apply=%region_11.12 | all-reduce | flops 24 | bytes 192 | tf_op jit(solution)/shard_map/psum | solution.py:43
  185.7 8.7 %all-reduce.1 = (f32[8]{0:T(128)S(1)}, f32[4,4]{1,0:T(4,128)S(1)}) all-reduce(f32[8]{0:T(128)S(1)} %get-tuple-element.13, f32[4,4]{1,0:T(4,128)S(1)} %get-tuple-element.14), channel_id=1, replica_groups=mesh['x'=4,'yh'=2,'z'=16,'yl'=2,'c'=2] {'x'}, use_global_device_ids=true, to_apply=%region_12.13 | all-reduce | flops 24 | bytes 192 | tf_op jit(solution)/shard_map/psum | solution.py:43
  194.4 24.3 %all-reduce = (f32[8]{0:T(128)S(1)}, f32[4,4]{1,0:T(4,128)S(1)}) all-reduce(f32[8]{0:T(128)S(1)} %get-tuple-element.7, f32[4,4]{1,0:T(4,128)S(1)} %get-tuple-element.8), channel_id=1, replica_groups=mesh['x'=4,'yh'=2,'z'=16,'yl'=2,'c'=2] {'z'}, use_global_device_ids=true, to_apply=%region_13.14 | all-reduce | flops 24 | bytes 192 | tf_op jit(solution)/shard_map/psum | solution.py:43
  218.7 0.1 broadcast_multiply_fusion.2
  218.7 0.2 exponential_reduce_fusion
  218.9 0.0 copy-done.2
  218.9 0.2 multiply_reduce_fusion.3
  219.2 0.1 multiply_multiply_fusion.5
  219.2 0.1 slice_multiply_fusion.1
  219.3 0.2 convolution_add_fusion.1
  219.5 0.3 convolution_add_fusion
  219.8 1.7 fusion.2
  221.5 0.8 copy.6
  222.3 0.0 all-gather.5.cloned.1.call-update
  222.3 0.0 reduce-scatter.9.cloned.1.call-start
  222.4 69.6 %all-gather.5.cloned.1.call-done = bf16[512,1536]{0,1:T(8,128)(2,1)} async-done(((bf16[512,192]{0,1:T(8,128)(2,1)}), bf16[512,1536]{0,1:T(8,128)(2,1)}) %all-gather.5.cloned.1.call-update) | async-done | bytes 1572880 | tf_op jit(solution)/shard_map/all_gather | solution.py:71
  292.0 4.6 %fusion.18 = f32[512,1024]{1,0:T(8,128)} fusion(bf16[512,1536]{0,1:T(8,128)(2,1)} %all-gather.5.cloned.1.call-done, bf16[1536,1024]{1,0:T(8,128)(2,1)S(1)} %copy-done), kind=kOutput, calls=%fused_computation.47 | convolution fusion | flops 1610612736 | bytes 6815744 | tf_op jit(solution)/shard_map/dot_general | solution.py:72
  296.5 0.0 reduce-scatter.9.cloned.1.call-update
  296.6 0.0 reduce-scatter.11.cloned.1.call-start
  296.6 63.7 %reduce-scatter.9.cloned.1.call-done = f32[32,1024]{1,0:T(8,128)} async-done(((f32[512,1024]{1,0:T(8,128)}), f32[32,1024]{1,0:T(8,128)}) %reduce-scatter.9.cloned.1.call-update) | async-done | bytes 131088 | tf_op jit(solution)/shard_map/reduce_scatter | solution.py:73
  360.3 0.0 reduce-scatter.11.cloned.1.call-update
  360.3 0.6 subtract_reduce_fusion
  360.9 35.8 %reduce-scatter.11.cloned.1.call-done = f32[8,1024]{1,0:T(8,128)} async-done(((f32[32,1024]{1,0:T(8,128)}), f32[8,1024]{1,0:T(8,128)}) %reduce-scatter.11.cloned.1.call-update) | async-done | bytes 32784 | tf_op jit(solution)/shard_map/reduce_scatter | solution.py:74
  (3 shorter events, 0.0 us)
Async XLA Ops:
  7.2 73.8 %copy-start = (bf16[1536,1024]{1,0:T(8,128)(2,1)S(1)}, bf16[1536,1024]{1,0:T(8,128)(2,1)}, u32[]{:S(2)}) copy-start(bf16[1536,1024]{1,0:T(8,128)(2,1)} %param.5) | copy-start | bytes 9437188
  7.2 73.8 %all-gather.3.cloned.1.call-start = ((), (), s32[]{:S(2)}) async-start(), calls=%async_computation.4 | async-start | bytes 1114112 | tf_op jit(solution)/shard_map/all_gather | solution.py:19
  20.0 118.3 %reduce-scatter.7.cloned.1.call-start = ((), (), s32[]{:S(2)}) async-start(), calls=%async_computation.5 | async-start | bytes 3932160 | tf_op jit(solution)/shard_map/reduce_scatter | solution.py:25
  85.7 54.9 %copy-start.1 = (s32[8]{0:T(128)S(1)}, s32[8]{0:T(128)}, u32[]{:S(2)}) copy-start(s32[8]{0:T(128)} %param.6) | copy-start | bytes 100
  85.7 133.2 %copy-start.2 = (s32[4]{0:T(128)S(1)}, s32[4]{0:T(128)}, u32[]{:S(2)}) copy-start(s32[4]{0:T(128)} %param.7) | copy-start | bytes 52
  85.7 84.3 %reduce-scatter.13.cloned.1.call-start = ((), (), s32[]{:S(2)}) async-start(), calls=%async_computation.9 | async-start | bytes 1179648
  140.6 151.4 %all-gather.5.cloned.1.call-start = ((), (), s32[]{:S(2)}) async-start(), calls=%async_computation.6 | async-start | bytes 1769472 | tf_op jit(solution)/shard_map/all_gather | solution.py:71
  222.3 137.9 %reduce-scatter.9.cloned.1.call-start = ((), (), s32[]{:S(2)}) async-start(), calls=%async_computation.7 | async-start | bytes 2228224 | tf_op jit(solution)/shard_map/reduce_scatter | solution.py:73
  296.6 100.1 %reduce-scatter.11.cloned.1.call-start = ((), (), s32[]{:S(2)}) async-start(), calls=%async_computation.8 | async-start | bytes 163840 | tf_op jit(solution)/shard_map/reduce_scatter | solution.py:74
Sparse Core Ops, SparseCore 0:
  20.1 60.8 all-gather.2
  85.9 52.3 reduce-scatter.6
  141.1 28.9 reduce-scatter.12
  222.5 69.4 all-gather.4
  296.7 63.5 reduce-scatter.8
  363.7 32.9 reduce-scatter.10
where the time goes:
time: 404 us
  waiting for transfers between devices  312 us (77%)
  blocking collectives  57.5 us (14%)
  between operations  14.2 us (4%)
  matrix products  9.88 us (2%)
  local copies, waits for them, and re-layouts  5.15 us (1%)
  other arithmetic  4.75 us (1%)
    all_gather x1, waiting for transfers between devices, local(): dlogit = lax.all_gather(dlogit, SEC, axis=1, tiled=True)  69.6 us
    reduce_scatter x1, waiting for transfers between devices, local(): lax.psum_scatter(partial_grad, 'z', scatter_dimension=0, tiled=True)  63.7 us
    all_gather x1, waiting for transfers between devices, local(): gathered = lax.all_gather(gathered, 'z', axis=0, tiled=True)  60.9 us
    reduce_scatter x1, waiting for transfers between devices, local(): lax.psum_scatter(partial_logits, 'x', scatter_dimension=1, tiled=True)  52.5 us
    psum x5, blocking collectives, local(): stats = lax.psum(stats, axis)  44.8 us
    reduce_scatter x1, waiting for transfers between devices, local(): lax.psum_scatter(hidden_grad, ('yl', 'c'), scatter_dimension=0, tiled=True)  35.8 us
    unnamed x7, waiting for transfers between devices  29.3 us
    all_gather x1, blocking collectives, local(): gathered = lax.all_gather(hidden, ('yl', 'c'), axis=0, tiled=True)  12.7 us
  transfers between devices with their start and end apart: 6, of which 6 were waited for; matrix products, arithmetic and copies ran while one was open for 0% of the time, Pallas kernels for 0%

commit v1 on v0

--- a/solution.py
+++ b/solution.py
@@ -68,7 +68,9 @@
     dpooled = jnp.concatenate([dpool_q, dpool_d], axis=0)
     dact = (dpooled[:, None, :] * expo / totals[:, None, :]).reshape(total_rows, columns)
     dlogit = (dact * jax.nn.sigmoid(logits) / (1.0 + soft)).astype(jnp.bfloat16)
-    dlogit = lax.all_gather(dlogit, SEC, axis=1, tiled=True)
+    dlogit = jnp.concatenate(
+        lax.all_to_all(jnp.stack([dlogit] * lax.axis_size(SEC)), SEC, 0, 0), axis=1
+    )
     partial_grad = jnp.dot(dlogit, head_weight, preferred_element_type=jnp.float32)
     hidden_grad = lax.psum_scatter(partial_grad, "z", scatter_dimension=0, tiled=True)
     hidden_grad = lax.psum_scatter(hidden_grad, ("yl", "c"), scatter_dimension=0, tiled=True)

time: 404 us -> 356 us (0.88)
  waiting for transfers between devices: 312 us -> 248 us
  blocking collectives: 57.5 us -> 74.3 us
    all_gather x1 -> x0, waiting for transfers between devices: 69.6 us -> none  [local(): dlogit = lax.all_gather(dlogit, SEC, axis=1, tiled=True)]
    all_to_all x0 -> x1, blocking collectives: none -> 16.7 us  [local(): lax.all_to_all(jnp.stack([dlogit] * lax.axis_size(SEC)), SEC, 0, 0)]
    reduce_scatter x1, waiting for transfers between devices: 63.7 us -> 69 us  [local(): lax.psum_scatter(partial_grad, 'z', scatter_dimension=0, tiled=True)]
    unnamed x7 -> x6, waiting for transfers between devices: 29.3 us -> 29.3 us
  transfers between devices with their start and end apart: 6 -> 5, of which waited for: 6 -> 5; matrix products, arithmetic and copies ran while one was open for 0% -> 0% of each run, Pallas kernels for 0% -> 0%
where the time goes in v1:
time: 356 us; the launch traced here: 355 us
  waiting for transfers between devices  248 us (70%)
  blocking collectives  74.3 us (21%)
  between operations  13.8 us (4%)
  matrix products  8.51 us (2%)
  local copies, waits for them, and re-layouts  5.56 us (2%)
  other arithmetic  5.45 us (2%)
    reduce_scatter x1, waiting for transfers between devices, local(): lax.psum_scatter(partial_grad, 'z', scatter_dimension=0, tiled=True)  69 us
    all_gather x1, waiting for transfers between devices, local(): gathered = lax.all_gather(gathered, 'z', axis=0, tiled=True)  60.9 us
    reduce_scatter x1, waiting for transfers between devices, local(): lax.psum_scatter(partial_logits, 'x', scatter_dimension=1, tiled=True)  52.5 us
    psum x5, blocking collectives, local(): stats = lax.psum(stats, axis)  44.8 us
    reduce_scatter x1, waiting for transfers between devices, local(): lax.psum_scatter(hidden_grad, ('yl', 'c'), scatter_dimension=0, tiled=True)  35.8 us
    unnamed x6, waiting for transfers between devices  29.3 us
    all_to_all x1, blocking collectives, local(): lax.all_to_all(jnp.stack([dlogit] * lax.axis_size(SEC)), SEC, 0, 0)  16.7 us
    all_gather x1, blocking collectives, local(): gathered = lax.all_gather(hidden, ('yl', 'c'), axis=0, tiled=True)  12.7 us
  transfers between devices with their start and end apart: 5, of which 5 were waited for; matrix products, arithmetic and copies ran while one was open for 0% of the time, Pallas kernels for 0%

profile of v1, /device:TPU:1, one launch (start us, length us, event | category | flops | bytes accessed | tf_op | source)
XLA Modules:
  0.0 355.4 jit_solution(3072520995899389020)
XLA Ops:
  7.2 0.0 copy-start
  7.2 0.0 all-gather.2.cloned.1.call-start
  7.2 12.7 %all_gather.6 = bf16[32,1024]{1,0:T(8,128)(2,1)} all-gather(bf16[8,1024]{1,0:T(8,128)(2,1)} %param.4), channel_id=1, replica_groups=mesh['x'=4,'yh'=2,'z'=16,'yl'=2,'c'=2] {'yl','c'}, dimensions={0}, use_global_device_ids=true | all-gather | bytes 81920 | tf_op jit(solution)/shard_map/all_gather | solution.py:18
  20.0 0.0 all-gather.2.cloned.1.call-update
  20.0 0.0 reduce-scatter.7.cloned.1.call-start
  20.0 60.9 %all-gather.2.cloned.1.call-done = bf16[512,1024]{1,0:T(8,128)(2,1)} async-done(((bf16[32,1024]{1,0:T(8,128)(2,1)}), bf16[512,1024]{1,0:T(8,128)(2,1)}) %all-gather.2.cloned.1.call-update) | async-done | bytes 1048592 | tf_op jit(solution)/shard_map/all_gather | solution.py:19
  81.0 0.0 copy-done
  81.0 4.7 %fusion.17 = f32[512,1536]{1,0:T(8,128)} fusion(bf16[512,1024]{1,0:T(8,128)(2,1)} %all-gather.2.cloned.1.call-done, bf16[1536,1024]{1,0:T(8,128)(2,1)S(1)} %copy-done), kind=kOutput, calls=%fused_computation.46 | convolution fusion | flops 1610612736 | bytes 7340032 | tf_op jit(solution)/shard_map/dot_general | solution.py:20
  85.7 0.0 copy-start.1
  85.7 0.0 copy-start.2
  85.7 0.0 reduce-scatter.7.cloned.1.call-update
  85.7 0.0 reduce-scatter.13.cloned.1.call-start
  85.8 52.5 %reduce-scatter.7.cloned.1.call-done = f32[512,384]{1,0:T(8,128)} async-done(((f32[512,1536]{1,0:T(8,128)}), f32[512,384]{1,0:T(8,128)}) %reduce-scatter.7.cloned.1.call-update) | async-done | bytes 786448 | tf_op jit(solution)/shard_map/reduce_scatter | solution.py:25
  138.3 2.3 copy.8
  140.6 0.0 reduce-scatter.13.cloned.1.call-update
  140.6 0.0 reduce-scatter.9.cloned.1.call-start
  140.6 0.0 copy-done.1
  140.6 0.1 fusion.3
  140.7 0.1 reshape.60
  140.8 29.2 %reduce-scatter.13.cloned.1.call-done = f32[192,512]{1,0:T(8,128)} async-done(((f32[384,512]{1,0:T(8,128)}), f32[192,512]{1,0:T(8,128)}) %reduce-scatter.13.cloned.1.call-update) | async-done | bytes 393232
  170.0 2.0 copy.9
  172.0 1.6 multiply_reduce_fusion
  173.6 0.1 multiply_reduce_fusion.1
  173.7 0.1 fusion.5
  173.9 2.8 all-reduce.2
  176.6 3.8 %all-reduce.3 = (f32[8]{0:T(128)S(1)}, f32[4,4]{1,0:T(4,128)S(1)}) all-reduce(f32[8]{0:T(128)S(1)} %get-tuple-element.9, f32[4,4]{1,0:T(4,128)S(1)} %get-tuple-element.10), channel_id=1, replica_groups=mesh['x'=4,'yh'=2,'z'=16,'yl'=2,'c'=2] {'yl'}, use_global_device_ids=true, to_apply=%region_10.11 | all-reduce | flops 24 | bytes 192 | tf_op jit(solution)/shard_map/psum | solution.py:43
  180.4 5.3 %all-reduce.4 = (f32[8]{0:T(128)S(1)}, f32[4,4]{1,0:T(4,128)S(1)}) all-reduce(f32[8]{0:T(128)S(1)} %get-tuple-element.11, f32[4,4]{1,0:T(4,128)S(1)} %get-tuple-element.12), channel_id=1, replica_groups=mesh['x'=4,'yh'=2,'z'=16,'yl'=2,'c'=2] {'yh'}, use_global_device_ids=true, to_apply=%region_11.12 | all-reduce | flops 24 | bytes 192 | tf_op jit(solution)/shard_map/psum | solution.py:43
  185.7 8.7 %all-reduce.1 = (f32[8]{0:T(128)S(1)}, f32[4,4]{1,0:T(4,128)S(1)}) all-reduce(f32[8]{0:T(128)S(1)} %get-tuple-element.13, f32[4,4]{1,0:T(4,128)S(1)} %get-tuple-element.14), channel_id=1, replica_groups=mesh['x'=4,'yh'=2,'z'=16,'yl'=2,'c'=2] {'x'}, use_global_device_ids=true, to_apply=%region_12.13 | all-reduce | flops 24 | bytes 192 | tf_op jit(solution)/shard_map/psum | solution.py:43
  194.4 24.3 %all-reduce = (f32[8]{0:T(128)S(1)}, f32[4,4]{1,0:T(4,128)S(1)}) all-reduce(f32[8]{0:T(128)S(1)} %get-tuple-element.7, f32[4,4]{1,0:T(4,128)S(1)} %get-tuple-element.8), channel_id=1, replica_groups=mesh['x'=4,'yh'=2,'z'=16,'yl'=2,'c'=2] {'z'}, use_global_device_ids=true, to_apply=%region_13.14 | all-reduce | flops 24 | bytes 192 | tf_op jit(solution)/shard_map/psum | solution.py:43
  218.7 0.1 broadcast_multiply_fusion.2
  218.7 0.2 exponential_reduce_fusion
  218.9 0.0 copy-done.2
  218.9 0.2 multiply_reduce_fusion.3
  219.2 0.1 multiply_multiply_fusion.5
  219.2 0.1 slice_multiply_fusion.1
  219.3 0.2 convolution_add_fusion.1
  219.5 0.3 convolution_add_fusion
  219.8 2.4 fusion.2
  222.2 1.1 copy.7
  223.3 0.1 stack.2
  223.4 16.7 %all_to_all.5 = bf16[8,512,192]{1,2,0:T(8,128)(2,1)S(1)} all-to-all(bf16[8,512,192]{1,2,0:T(8,128)(2,1)S(1)} %stack.2), channel_id=1, replica_groups=mesh['x'=4,'yh'=2,'z'=16,'yl'=2,'c'=2] {'x','yh'}, dimensions={0} | all-to-all | bytes 3145728 | tf_op jit(solution)/shard_map/all_to_all | solution.py:72
  240.2 3.2 fusion.18
  243.4 0.0 reduce-scatter.9.cloned.1.call-update
  243.4 0.0 reduce-scatter.11.cloned.1.call-start
  243.5 69.0 %reduce-scatter.9.cloned.1.call-done = f32[32,1024]{1,0:T(8,128)} async-done(((f32[512,1024]{1,0:T(8,128)}), f32[32,1024]{1,0:T(8,128)}) %reduce-scatter.9.cloned.1.call-update) | async-done | bytes 131088 | tf_op jit(solution)/shard_map/reduce_scatter | solution.py:75
  312.4 0.0 reduce-scatter.11.cloned.1.call-update
  312.4 0.6 subtract_reduce_fusion
  313.1 35.8 %reduce-scatter.11.cloned.1.call-done = f32[8,1024]{1,0:T(8,128)} async-done(((f32[32,1024]{1,0:T(8,128)}), f32[8,1024]{1,0:T(8,128)}) %reduce-scatter.11.cloned.1.call-update) | async-done | bytes 32784 | tf_op jit(solution)/shard_map/reduce_scatter | solution.py:76
  (3 shorter events, 0.0 us)
Async XLA Ops:
  7.2 73.8 %copy-start = (bf16[1536,1024]{1,0:T(8,128)(2,1)S(1)}, bf16[1536,1024]{1,0:T(8,128)(2,1)}, u32[]{:S(2)}) copy-start(bf16[1536,1024]{1,0:T(8,128)(2,1)} %param.5) | copy-start | bytes 9437188
  7.2 73.8 %all-gather.2.cloned.1.call-start = ((), (), s32[]{:S(2)}) async-start(), calls=%async_computation.5 | async-start | bytes 1114112 | tf_op jit(solution)/shard_map/all_gather | solution.py:19
  20.0 118.3 %reduce-scatter.7.cloned.1.call-start = ((), (), s32[]{:S(2)}) async-start(), calls=%async_computation.6 | async-start | bytes 3932160 | tf_op jit(solution)/shard_map/reduce_scatter | solution.py:25
  85.7 54.9 %copy-start.1 = (s32[8]{0:T(128)S(1)}, s32[8]{0:T(128)}, u32[]{:S(2)}) copy-start(s32[8]{0:T(128)} %param.6) | copy-start | bytes 100
  85.7 133.2 %copy-start.2 = (s32[4]{0:T(128)S(1)}, s32[4]{0:T(128)}, u32[]{:S(2)}) copy-start(s32[4]{0:T(128)} %param.7) | copy-start | bytes 52
  85.7 84.3 %reduce-scatter.13.cloned.1.call-start = ((), (), s32[]{:S(2)}) async-start(), calls=%async_computation.9 | async-start | bytes 1179648
  140.6 171.8 %reduce-scatter.9.cloned.1.call-start = ((), (), s32[]{:S(2)}) async-start(), calls=%async_computation.7 | async-start | bytes 2228224 | tf_op jit(solution)/shard_map/reduce_scatter | solution.py:75
  243.4 105.5 %reduce-scatter.11.cloned.1.call-start = ((), (), s32[]{:S(2)}) async-start(), calls=%async_computation.8 | async-start | bytes 163840 | tf_op jit(solution)/shard_map/reduce_scatter | solution.py:76
Sparse Core Ops, SparseCore 0:
  20.1 60.8 all-gather.1
  85.9 52.3 reduce-scatter.6
  141.1 28.9 reduce-scatter.12
  243.5 68.8 reduce-scatter.8
  315.9 32.9 reduce-scatter.10
